TPU v7x, 32 devices: a whole 2x2x4 slice. The times are simulated.
32 devices in a mesh: groups: 2 (over x), rows: 16 (over z, y, core).
Axes of the slice: x: 2, y: 2, z: 4, core: 2. Of those that a mesh axis runs over, the one named last changes fastest.
Arguments:
- student: float32 [8192, 512], P(('groups', 'rows')), parts along dimension 0, may hold values from -6 to 6
- teacher: float32 [8192, 6144], P(('groups', 'rows')), parts along dimension 0, may hold values from -6 to 6
- heads: bfloat16 [512, 6144], P(None, 'rows'), may hold values from -0.25 to 0.25
Outputs:
- grad_student: float32 [8192, 512], P(('groups', 'rows')), parts along dimension 0
- grad_heads: float32 [1024, 6144], P('groups', 'rows'), parts along dimension 0
There are 2 independent parts, one for each index of `groups`. A program takes and returns all parts, laid end to end along the dimension named above; an argument that names none is the same for every part. Nothing has to cross between parts.
All inputs are finite; a program needn't handle non-finite values.
Results may differ from a plain program's by a relative error of at most 0.0026.
Values may be sent and summed in bfloat16 or wider, within the bound.
No kernel may reach another device: no remote copies, remote signals or barrier semaphores. Data moves between devices by JAX's collectives and lax.ppermute only.
A program may use at most 128 MiB of HBM per device.

v0:
```python
import jax
import jax.numpy as jnp
from jax import lax
from jax.sharding import PartitionSpec as P

reg_weight = 0.0625
head_scale = 0.015625


def contract(left, right, left_dim, right_dim):
    return lax.dot_general(
        left,
        right,
        (((left_dim,), (right_dim,)), ((), ())),
        precision=lax.Precision.HIGHEST,
        preferred_element_type=jnp.float32,
    )


def per_device(student, teacher, heads):
    devices = lax.axis_size("rows")
    rows_here, model_width = student.shape
    total_rows = rows_here * devices
    positions = jnp.arange(model_width)
    weights = (
        1.0
        + (positions < model_width // 4).astype(jnp.float32)
        + (positions < model_width // 2).astype(jnp.float32)
    )
    nested = jnp.minimum(weights[:, None], weights[None, :])
    gram_scale = 0.5 / total_rows
    wide_here = heads.astype(jnp.float32)
    moment = lax.psum(contract(student, student, 0, 0), "rows")
    cross_here = lax.psum_scatter(
        contract(teacher, student, 0, 0), "rows", scatter_dimension=0, tiled=True
    )
    grad_heads = head_scale * (contract(moment, wide_here, 1, 0) - cross_here.T)
    cross_sent = cross_here.T.astype(jnp.bfloat16)
    gathered = (
        lax.all_gather(heads, "rows", axis=1, tiled=True),
        lax.all_gather(cross_sent, "rows", axis=1, tiled=True),
    )
    wide_all = gathered[0].astype(jnp.float32)
    cross_all = gathered[1].astype(jnp.float32)
    error = contract(student, wide_all, 1, 0) - teacher
    shared = (
        reg_weight * contract(error, wide_all, 1, 1)
        - gram_scale * contract(teacher, cross_all, 1, 1) * weights[None, :]
    )
    grad_student = shared + gram_scale * contract(student, moment * nested, 1, 0)
    return (grad_student, grad_heads)


def solution(mesh):
    in_specs = (P(("groups", "rows"), None), P(("groups", "rows"), None), P(None, "rows"))
    out_specs = (P(("groups", "rows"), None), P("groups", "rows"))
    return jax.shard_map(
        per_device, mesh=mesh, in_specs=in_specs, out_specs=out_specs, check_vma=False
    )
```

profile of v0, /device:TPU:0, one launch (start us, length us, event | category | flops | bytes accessed | tf_op | source)
XLA Modules:
  0.0 414.8 jit_solution(12258084241356141119)
XLA Ops:
  7.2 0.0 copy-start
  7.2 0.0 reduce-scatter.2.cloned.1.call-start
  7.2 1.0 copy-done
  8.2 14.8 %fusion.9 = f32[6144,512]{1,0:T(8,128)} fusion(f32[256,6144]{1,0:T(8,128)} %param.4, f32[256,512]{1,0:T(8,128)S(1)} %copy-done), kind=kOutput, calls=%fused_computation.19 | convolution fusion | flops 9663676416 | bytes 19398656 | tf_op jit(solution)/shard_map/dot_general | solution.py:11
  23.0 0.0 reduce-scatter.2.cloned.1.call-update
  23.0 0.0 all-gather.3.cloned.1.call-start
  23.0 0.7 all-gather.3.cloned.1.call-update
  23.8 0.0 all-reduce.2.cloned.1.call-start
  23.8 2.0 fusion.10
  25.8 0.0 all-reduce.2.cloned.1.call-update
  25.9 0.2 all-gather.5.cloned.1.call-start
  26.1 134.4 %reduce-scatter.2.cloned.1.call-done = f32[384,512]{1,0:T(8,128)} async-done(((f32[6144,512]{1,0:T(8,128)}), f32[384,512]{1,0:T(8,128)}) %reduce-scatter.2.cloned.1.call-update) | async-done | bytes 786448 | tf_op jit(solution)/shard_map/reduce_scatter | solution.py:34
  160.5 1.9 bitcast_convert_fusion
  162.4 0.0 all-gather.5.cloned.1.call-update
  162.4 0.0 copy-start.2
  162.5 0.0 copy-start.3
  162.5 65.0 %all-gather.3.cloned.1.call-done = bf16[512,6144]{1,0:T(8,128)(2,1)} async-done(((bf16[512,384]{1,0:T(8,128)(2,1)}), bf16[512,6144]{1,0:T(8,128)(2,1)}) %all-gather.3.cloned.1.call-update) | async-done | bytes 6291472 | tf_op jit(solution)/shard_map/all_gather | solution.py:40
  227.5 10.7 %convolution_subtract_fusion = f32[256,6144]{1,0:T(8,128)} fusion(f32[256,6144]{1,0:T(8,128)} %param.4, f32[256,512]{1,0:T(8,128)S(1)} %copy-done, bf16[512,6144]{1,0:T(8,128)(2,1)} %all-gather.3.cloned.1.call-done), kind=kOutput, calls=%fused_computation | convolution fusion | flops 9665249280 | bytes 19398656 | tf_op jit(solution)/shard_map/dot_general | solution.py:11
  238.2 84.2 %all-reduce.2.cloned.1.call-done = f32[512,512]{1,0:T(8,128)} async-done(((f32[512,512]{1,0:T(8,128)}), f32[512,512]{1,0:T(8,128)}) %all-reduce.2.cloned.1.call-update) | async-done | bytes 1048592 | tf_op jit(solution)/shard_map/psum | solution.py:33
  322.4 0.0 copy-done.2
  322.4 0.0 copy-done.3
  322.4 2.1 fusion
  324.5 1.1 copy.8
  325.7 60.6 %all-gather.5.cloned.1.call-done = bf16[512,6144]{0,1:T(8,128)(2,1)} async-done(((bf16[512,384]{0,1:T(8,128)(2,1)}), bf16[512,6144]{0,1:T(8,128)(2,1)}) %all-gather.5.cloned.1.call-update) | async-done | bytes 6291472 | tf_op jit(solution)/shard_map/all_gather | solution.py:41
  386.3 9.8 %fusion.3 = f32[256,512]{1,0:T(8,128)S(1)} fusion(bf16[512,6144]{0,1:T(8,128)(2,1)} %all-gather.5.cloned.1.call-done, f32[256,6144]{1,0:T(8,128)} %param.4, f32[512]{0:T(512)S(1)} %broadcast_multiply_fusion), kind=kOutput, calls=%fused_computation.7 | convolution fusion | flops 9663807488 | bytes 13109248 | tf_op jit(solution)/shard_map/dot_general | solution.py:11
  396.1 0.0 copy-start.1
  396.1 10.1 %fusion.4 = f32[256,512]{1,0:T(8,128)S(1)} fusion(f32[256,512]{1,0:T(8,128)S(1)} %fusion.3, f32[256,6144]{1,0:T(8,128)} %convolution_subtract_fusion, bf16[512,6144]{1,0:T(8,128)(2,1)} %all-gather.3.cloned.1.call-done), kind=kOutput, calls=%fused_computation.9 | convolution fusion | flops 9663938560 | bytes 13631488 | tf_op jit(solution)/shard_map/dot_general | solution.py:11
  406.2 0.0 copy-done.1
  406.2 2.1 fusion.2
  (2 shorter events, 0.0 us)
Async XLA Ops:
  7.2 1.0 copy-start
  7.2 153.3 %reduce-scatter.2.cloned.1.call-start = ((), (), s32[]{:S(2)}) async-start(), calls=%async_computation.2 | async-start | bytes 13369344 | tf_op jit(solution)/shard_map/reduce_scatter | solution.py:34
  23.0 204.5 %all-gather.3.cloned.1.call-start = ((), (), s32[]{:S(2)}) async-start(), calls=%async_computation.1 | async-start | bytes 6684672 | tf_op jit(solution)/shard_map/all_gather | solution.py:40
  23.8 298.7 %all-reduce.2.cloned.1.call-start = ((), (), s32[]{:S(2)}) async-start(), calls=%async_computation.4 | async-start | bytes 2097152 | tf_op jit(solution)/shard_map/psum | solution.py:33
  25.9 360.4 %all-gather.5.cloned.1.call-start = ((), (), s32[]{:S(2)}) async-start(), calls=%async_computation.3 | async-start | bytes 6684672 | tf_op jit(solution)/shard_map/all_gather | solution.py:41
  162.4 160.0 %copy-start.2 = (f32[384,512]{1,0:T(8,128)S(1)}, f32[384,512]{1,0:T(8,128)}, u32[]{:S(2)}) copy-start(f32[384,512]{1,0:T(8,128)} %reduce-scatter.2.cloned.1.call-done) | copy-start | bytes 2359300
  162.5 160.0 %copy-start.3 = (bf16[512,384]{1,0:T(8,128)(2,1)S(1)}, bf16[512,384]{1,0:T(8,128)(2,1)}, u32[]{:S(2)}) copy-start(bf16[512,384]{1,0:T(8,128)(2,1)} %param.5) | copy-start | bytes 1179652
  396.1 10.1 %copy-start.1 = (f32[512,512]{1,0:T(8,128)S(1)}, f32[512,512]{1,0:T(8,128)}, u32[]{:S(2)}) copy-start(f32[512,512]{1,0:T(8,128)} %all-reduce.2.cloned.1.call-done) | copy-start | bytes 3145732
Sparse Core Ops, SparseCore 0:
  23.1 137.3 reduce-scatter.1
  162.6 64.7 all-gather.2
  230.9 91.4 all-reduce.1
  325.1 61.0 all-gather.4
where the time goes:
time: 415 us
  waiting for transfers between devices  345 us (83%)
  matrix products  51.6 us (12%)
  between operations  13.8 us (3%)
    reduce_scatter x1, waiting for transfers between devices, per_device(): lax.psum_scatter(contract(teacher, student, 0, 0), 'rows', scatter_dimens...  134 us
    psum x1, waiting for transfers between devices, per_device(): moment = lax.psum(contract(student, student, 0, 0), 'rows')  84.2 us
    all_gather x1, waiting for transfers between devices, per_device(): lax.all_gather(heads, 'rows', axis=1, tiled=True)  65 us
    all_gather x1, waiting for transfers between devices, per_device(): lax.all_gather(cross_sent, 'rows', axis=1, tiled=True)  60.6 us
    dot_general x7, matrix products, contract(): lax.dot_general(left, right, (((left_dim,), (right_dim,)), ((), ())), pre...  51.6 us
  transfers between devices with their start and end apart: 4, of which 4 were waited for; matrix products, arithmetic and copies ran while one was open for 4% of the time, Pallas kernels for 0%

commit v1 on v0

--- a/solution.py
+++ b/solution.py
@@ -5,6 +5,27 @@
 
 reg_weight = 0.0625
 head_scale = 0.015625
+
+
+def ring_gather(x, axis, dim):
+    count, place, extent = (lax.axis_size(axis), lax.axis_index(axis), x.shape[dim])
+    right = [(i, (i + 1) % count) for i in range(count)]
+    left = [(i, (i - 1) % count) for i in range(count)]
+    filled = jnp.zeros((*x.shape[:dim], count * extent, *x.shape[dim + 1 :]), x.dtype)
+    filled = lax.dynamic_update_slice_in_dim(filled, x, place * extent, axis=dim)
+    from_left = from_right = x
+    half = count // 2
+    for step in range(1, half + 1):
+        from_left = lax.ppermute(from_left, axis, right)
+        filled = lax.dynamic_update_slice_in_dim(
+            filled, from_left, (place - step) % count * extent, axis=dim
+        )
+        if step < count - half:
+            from_right = lax.ppermute(from_right, axis, left)
+            filled = lax.dynamic_update_slice_in_dim(
+                filled, from_right, (place + step) % count * extent, axis=dim
+            )
+    return filled
 
 
 def contract(left, right, left_dim, right_dim):
@@ -38,7 +59,7 @@
     cross_sent = cross_here.T.astype(jnp.bfloat16)
     gathered = (
         lax.all_gather(heads, "rows", axis=1, tiled=True),
-        lax.all_gather(cross_sent, "rows", axis=1, tiled=True),
+        ring_gather(cross_sent, "rows", 1),
     )
     wide_all = gathered[0].astype(jnp.float32)
     cross_all = gathered[1].astype(jnp.float32)

time: 415 us -> 395 us (0.952)
  waiting for transfers between devices: 345 us -> 273 us
  starting transfers between devices: 0.34 us -> 32.7 us
  local copies, waits for them, and re-layouts: 2.16 us -> 27.2 us
  matrix products: 51.6 us -> 46.4 us
    all_gather x1 -> x0, waiting for transfers between devices: 60.6 us -> none  [per_device(): lax.all_gather(cross_sent, 'rows', axis=1, tiled=True)]
    ppermute x0 -> x15, starting transfers between devices: none -> 32.6 us  [the longest x7 22.2 us: ring_gather(): from_right = lax.ppermute(from_right, axis, left)]
    dynamic_update_slice x0 -> x15, local copies, waits for them, and re-layouts: none -> 20.8 us  [the longest x8 11.4 us: ring_gather(): lax.dynamic_update_slice_in_dim(filled, from_left, (place - step) % count...]
    all_gather x1, waiting for transfers between devices: 65 us -> 46.9 us  [per_device(): lax.all_gather(heads, 'rows', axis=1, tiled=True)]
    ppermute x0 -> x15, waiting for transfers between devices: none -> 15.4 us  [the longest x8 12.5 us: ring_gather(): from_left = lax.ppermute(from_left, axis, right)]
    psum x1, waiting for transfers between devices: 84.2 us -> 73.3 us  [per_device(): moment = lax.psum(contract(student, student, 0, 0), 'rows')]
    dot_general x7, matrix products: 51.6 us -> 46.4 us  [contract(): lax.dot_general(left, right, (((left_dim,), (right_dim,)), ((), ())), pre...]
  transfers between devices with their start and end apart: 4 -> 18, of which waited for: 4 -> 9; matrix products, arithmetic and copies ran while one was open for 4% -> 12% of each run, Pallas kernels for 0% -> 0%
where the time goes in v1:
time: 395 us; the launch traced here: 394 us
  waiting for transfers between devices  273 us (69%)
  matrix products  46.4 us (12%)
  starting transfers between devices  32.7 us (8%)
  local copies, waits for them, and re-layouts  27.2 us (7%)
  between operations  14.2 us (4%)
    reduce_scatter x1, waiting for transfers between devices, per_device(): lax.psum_scatter(contract(teacher, student, 0, 0), 'rows', scatter_dimens...  137 us
    psum x1, waiting for transfers between devices, per_device(): moment = lax.psum(contract(student, student, 0, 0), 'rows')  73.3 us
    all_gather x1, waiting for transfers between devices, per_device(): lax.all_gather(heads, 'rows', axis=1, tiled=True)  46.9 us
    dot_general x7, matrix products, contract(): lax.dot_general(left, right, (((left_dim,), (right_dim,)), ((), ())), pre...  46.4 us
    ppermute x7, starting transfers between devices, ring_gather(): from_right = lax.ppermute(from_right, axis, left)  22.2 us
    ppermute x8, waiting for transfers between devices, ring_gather(): from_left = lax.ppermute(from_left, axis, right)  12.5 us
    dynamic_update_slice x8, local copies, waits for them, and re-layouts, ring_gather(): lax.dynamic_update_slice_in_dim(filled, from_left, (place - step) % count...  11.4 us
    ppermute x8, starting transfers between devices, ring_gather(): from_left = lax.ppermute(from_left, axis, right)  10.4 us
  transfers between devices with their start and end apart: 18, of which 9 were waited for; matrix products, arithmetic and copies ran while one was open for 12% of the time, Pallas kernels for 0%

profile of v1, /device:TPU:0, one launch (start us, length us, event | category | flops | bytes accessed | tf_op | source)
XLA Modules:
  0.0 394.4 jit_solution(17530857213697517297)
XLA Ops:
  7.2 0.0 copy-start
  7.2 0.0 reduce-scatter.2.cloned.1.call-start
  7.2 1.0 copy-done
  8.2 14.7 %fusion.9 = f32[6144,512]{1,0:T(8,128)} fusion(f32[256,6144]{1,0:T(8,128)} %param.4, f32[256,512]{1,0:T(8,128)S(1)} %copy-done), kind=kOutput, calls=%fused_computation.35 | convolution fusion | flops 9663676416 | bytes 19398656 | tf_op jit(solution)/shard_map/dot_general | solution.py:32
  22.9 0.0 reduce-scatter.2.cloned.1.call-update
  23.0 0.0 all-gather.2.cloned.1.call-start
  23.0 0.7 all-gather.2.cloned.1.call-update
  23.7 0.0 all-reduce.2.cloned.1.call-start
  23.8 136.7 %reduce-scatter.2.cloned.1.call-done = f32[384,512]{1,0:T(8,128)} async-done(((f32[6144,512]{1,0:T(8,128)}), f32[384,512]{1,0:T(8,128)}) %reduce-scatter.2.cloned.1.call-update) | async-done | bytes 786448 | tf_op jit(solution)/shard_map/reduce_scatter | solution.py:55
  160.4 3.0 broadcast_in_dim.2
  163.5 0.8 constant_dynamic-update-slice_fusion.15
  164.3 0.0 collective-permute-start
  164.3 4.4 %collective-permute-start.1 = (bf16[512,384]{0,1:T(8,128)(2,1)S(1)}, bf16[512,384]{0,1:T(8,128)(2,1)S(1)}, u32[]{:S(2)}, u32[]{:S(2)}) collective-permute-start(bf16[512,384]{0,1:T(8,128)(2,1)S(1)} %get-tuple-element.5), channel_id=1, source_target_pairs={{0,15},{1,0},{2,1},{3,2},{4,3},{5,4},{6,5},{7,6},{8,7},{9,8},{10,9... | collective-permute-start | bytes 1179656 | tf_op jit(solution)/shard_map/ppermute | solution.py:24
  168.7 5.6 %collective-permute-done = bf16[512,384]{0,1:T(8,128)(2,1)S(1)} collective-permute-done((bf16[512,384]{0,1:T(8,128)(2,1)S(1)}, bf16[512,384]{0,1:T(8,128)(2,1)S(1)}, u32[]{:S(2)}, u32[]{:S(2)}) %collective-permute-start) | collective-permute-done | bytes 393248 | tf_op jit(solution)/shard_map/ppermute | solution.py:19
  174.4 4.7 %collective-permute-start.2 = (bf16[512,384]{0,1:T(8,128)(2,1)S(1)}, bf16[512,384]{0,1:T(8,128)(2,1)S(1)}, u32[]{:S(2)}, u32[]{:S(2)}) collective-permute-start(bf16[512,384]{0,1:T(8,128)(2,1)S(1)} %collective-permute-done), channel_id=1, source_target_pairs={{0,1},{1,2},{2,3},{3,4},{4,5},{5,6},{6,7},{7,8},{8,9},{9,10},{10,1... | collective-permute-start | bytes 1179656 | tf_op jit(solution)/shard_map/ppermute | solution.py:19
  179.1 2.1 fusion.10
  181.2 0.0 all-reduce.2.cloned.1.call-update
  181.5 0.0 collective-permute-done.1
  181.6 1.4 collective-permute-start.3
  183.0 1.5 collective-permute-done.2
  184.5 5.6 %collective-permute-start.4 = (bf16[512,384]{0,1:T(8,128)(2,1)S(1)}, bf16[512,384]{0,1:T(8,128)(2,1)S(1)}, u32[]{:S(2)}, u32[]{:S(2)}) collective-permute-start(bf16[512,384]{0,1:T(8,128)(2,1)S(1)} %collective-permute-done.2), channel_id=1, source_target_pairs={{0,1},{1,2},{2,3},{3,4},{4,5},{5,6},{6,7},{7,8},{8,9},{9,10},{10,1... | collective-permute-start | bytes 1179656 | tf_op jit(solution)/shard_map/ppermute | solution.py:19
  190.1 46.9 %all-gather.2.cloned.1.call-done = bf16[512,6144]{1,0:T(8,128)(2,1)} async-done(((bf16[512,384]{1,0:T(8,128)(2,1)}), bf16[512,6144]{1,0:T(8,128)(2,1)}) %all-gather.2.cloned.1.call-update) | async-done | bytes 6291472 | tf_op jit(solution)/shard_map/all_gather | solution.py:61
  237.1 10.2 %convolution_subtract_fusion = f32[256,6144]{1,0:T(8,128)S(1)} fusion(f32[256,6144]{1,0:T(8,128)} %param.4, f32[256,512]{1,0:T(8,128)S(1)} %copy-done, bf16[512,6144]{1,0:T(8,128)(2,1)} %all-gather.2.cloned.1.call-done), kind=kOutput, calls=%fused_computation | convolution fusion | flops 9665249280 | bytes 19398656 | tf_op jit(solution)/shard_map/dot_general | solution.py:32
  247.3 0.0 collective-permute-done.3
  247.3 1.6 collective-permute-start.5
  248.9 0.0 collective-permute-done.4
  248.9 0.0 collective-permute-start.6
  248.9 5.9 %convolution_multiply_fusion.2 = f32[256,512]{1,0:T(8,128)} fusion(f32[256,6144]{1,0:T(8,128)S(1)} %convolution_subtract_fusion, bf16[512,6144]{1,0:T(8,128)(2,1)S(1)} %copy-done.1), kind=kOutput, calls=%fused_computation.8 | convolution fusion | flops 9663807488 | bytes 13107200 | tf_op jit(solution)/shard_map/dot_general | solution.py:32
  254.8 0.7 collective-permute-done.5
  255.5 4.7 %collective-permute-start.7 = (bf16[512,384]{0,1:T(8,128)(2,1)}, bf16[512,384]{0,1:T(8,128)(2,1)}, u32[]{:S(2)}, u32[]{:S(2)}) collective-permute-start(bf16[512,384]{0,1:T(8,128)(2,1)} %collective-permute-done.5), channel_id=1, source_target_pairs={{0,15},{1,0},{2,1},{3,2},{4,3},{5,4},{6,5},{7,6},{8,7},{9,8},{10,9... | collective-permute-start | bytes 1179656 | tf_op jit(solution)/shard_map/ppermute | solution.py:24
  260.3 0.7 collective-permute-done.6
  261.0 0.0 collective-permute-start.8
  261.0 73.3 %all-reduce.2.cloned.1.call-done = f32[512,512]{1,0:T(8,128)} async-done(((f32[512,512]{1,0:T(8,128)}), f32[512,512]{1,0:T(8,128)}) %all-reduce.2.cloned.1.call-update) | async-done | bytes 1048592 | tf_op jit(solution)/shard_map/psum | solution.py:54
  334.4 3.3 fusion
  337.7 2.3 copy.8
  339.9 1.8 constant_dynamic-update-slice_fusion.14
  341.8 0.0 collective-permute-done.7
  341.8 1.1 collective-permute-start.9
  342.9 1.8 constant_dynamic-update-slice_fusion.13
  344.7 0.0 collective-permute-done.8
  344.7 0.0 collective-permute-start.10
  344.7 1.8 constant_dynamic-update-slice_fusion.12
  346.4 1.8 constant_dynamic-update-slice_fusion.11
  348.2 1.9 constant_dynamic-update-slice_fusion.10
  350.2 0.0 collective-permute-done.9
  350.2 4.5 %collective-permute-start.11 = (bf16[512,384]{0,1:T(8,128)(2,1)S(1)}, bf16[512,384]{0,1:T(8,128)(2,1)S(1)}, u32[]{:S(2)}, u32[]{:S(2)}) collective-permute-start(bf16[512,384]{0,1:T(8,128)(2,1)S(1)} %collective-permute-done.9), channel_id=1, source_target_pairs={{0,15},{1,0},{2,1},{3,2},{4,3},{5,4},{6,5},{7,6},{8,7},{9,8},{10,9... | collective-permute-start | bytes 1179656 | tf_op jit(solution)/shard_map/ppermute | solution.py:24
  354.6 1.8 constant_dynamic-update-slice_fusion.9
  356.4 0.0 collective-permute-done.10
  356.4 0.0 collective-permute-start.12
  356.4 1.8 constant_dynamic-update-slice_fusion.8
  358.2 1.8 constant_dynamic-update-slice_fusion.7
  360.0 1.8 constant_dynamic-update-slice_fusion.6
  361.7 0.0 collective-permute-done.11
  361.7 4.4 %collective-permute-start.13 = (bf16[512,384]{0,1:T(8,128)(2,1)S(1)}, bf16[512,384]{0,1:T(8,128)(2,1)S(1)}, u32[]{:S(2)}, u32[]{:S(2)}) collective-permute-start(bf16[512,384]{0,1:T(8,128)(2,1)S(1)} %collective-permute-done.11), channel_id=1, source_target_pairs={{0,15},{1,0},{2,1},{3,2},{4,3},{5,4},{6,5},{7,6},{8,7},{9,8},{10,9... | collective-permute-start | bytes 1179656 | tf_op jit(solution)/shard_map/ppermute | solution.py:24
  366.2 0.8 constant_dynamic-update-slice_fusion.5
  367.0 0.8 constant_dynamic-update-slice_fusion.4
  367.8 0.8 constant_dynamic-update-slice_fusion.3
  368.5 0.8 constant_dynamic-update-slice_fusion.2
  369.3 2.2 collective-permute-done.13
  371.5 0.8 constant_dynamic-update-slice_fusion.1
  372.2 4.6 %collective-permute-done.14 = bf16[512,384]{0,1:T(8,128)(2,1)S(1)} collective-permute-done((bf16[512,384]{0,1:T(8,128)(2,1)S(1)}, bf16[512,384]{0,1:T(8,128)(2,1)S(1)}, u32[]{:S(2)}, u32[]{:S(2)}) %collective-permute-start.14) | collective-permute-done | bytes 393248 | tf_op jit(solution)/shard_map/ppermute | solution.py:19
  376.9 0.8 constant_dynamic-update-slice_fusion
  377.7 8.1 %fusion.4 = f32[256,512]{1,0:T(8,128)S(1)} fusion(f32[256,512]{1,0:T(8,128)S(1)} %copy-done.4, bf16[512,6144]{0,1:T(8,128)(2,1)} %constant_dynamic-update-slice_fusion, f32[256,6144]{1,0:T(8,128)S(1)} %bitcast.26, f32[512]{0:T(512)S(1)} %broadcast_multiply_fusion), kind=kOutput, calls=%fused_computation.9 | convolution fusion | flops 9663938560 | bytes 13633536 | tf_op jit(solution)/shard_map/dot_general | solution.py:32
  385.8 2.1 fusion.2
  (27 shorter events, 0.1 us)
Async XLA Ops:
  7.2 1.0 copy-start
  7.2 153.3 %reduce-scatter.2.cloned.1.call-start = ((), (), s32[]{:S(2)}) async-start(), calls=%async_computation.2 | async-start | bytes 13369344 | tf_op jit(solution)/shard_map/reduce_scatter | solution.py:55
  23.0 214.1 %all-gather.2.cloned.1.call-start = ((), (), s32[]{:S(2)}) async-start(), calls=%async_computation.1 | async-start | bytes 6684672 | tf_op jit(solution)/shard_map/all_gather | solution.py:61
  23.7 310.6 %all-reduce.2.cloned.1.call-start = ((), (), s32[]{:S(2)}) async-start(), calls=%async_computation.3 | async-start | bytes 2097152 | tf_op jit(solution)/shard_map/psum | solution.py:54
  160.4 3.0 copy-start.3
  164.3 10.1 %collective-permute-start = (bf16[512,384]{0,1:T(8,128)(2,1)S(1)}, bf16[512,384]{0,1:T(8,128)(2,1)S(1)}, u32[]{:S(2)}, u32[]{:S(2)}) collective-permute-start(bf16[512,384]{0,1:T(8,128)(2,1)S(1)} %get-tuple-element.5), channel_id=1, source_target_pairs={{0,1},{1,2},{2,3},{3,4},{4,5},{5,6},{6,7},{7,8},{8,9},{9,10},{10,1... | collective-permute-start | bytes 1179656 | tf_op jit(solution)/shard_map/ppermute | solution.py:19
  164.3 17.2 %collective-permute-start.1 = (bf16[512,384]{0,1:T(8,128)(2,1)S(1)}, bf16[512,384]{0,1:T(8,128)(2,1)S(1)}, u32[]{:S(2)}, u32[]{:S(2)}) collective-permute-start(bf16[512,384]{0,1:T(8,128)(2,1)S(1)} %get-tuple-element.5), channel_id=1, source_target_pairs={{0,15},{1,0},{2,1},{3,2},{4,3},{5,4},{6,5},{7,6},{8,7},{9,8},{10,9... | collective-permute-start | bytes 1179656 | tf_op jit(solution)/shard_map/ppermute | solution.py:24
  174.3 72.9 %copy-start.7 = (bf16[512,384]{0,1:T(8,128)(2,1)}, bf16[512,384]{0,1:T(8,128)(2,1)S(1)}, u32[]{:S(2)}) copy-start(bf16[512,384]{0,1:T(8,128)(2,1)S(1)} %collective-permute-done) | copy-start | bytes 1179652
  174.4 10.1 %collective-permute-start.2 = (bf16[512,384]{0,1:T(8,128)(2,1)S(1)}, bf16[512,384]{0,1:T(8,128)(2,1)S(1)}, u32[]{:S(2)}, u32[]{:S(2)}) collective-permute-start(bf16[512,384]{0,1:T(8,128)(2,1)S(1)} %collective-permute-done), channel_id=1, source_target_pairs={{0,1},{1,2},{2,3},{3,4},{4,5},{5,6},{6,7},{7,8},{8,9},{9,10},{10,1... | collective-permute-start | bytes 1179656 | tf_op jit(solution)/shard_map/ppermute | solution.py:19
  181.5 65.8 %copy-start.6 = (bf16[512,384]{0,1:T(8,128)(2,1)}, bf16[512,384]{0,1:T(8,128)(2,1)S(1)}, u32[]{:S(2)}) copy-start(bf16[512,384]{0,1:T(8,128)(2,1)S(1)} %collective-permute-done.1) | copy-start | bytes 1179652
  181.6 65.8 %collective-permute-start.3 = (bf16[512,384]{0,1:T(8,128)(2,1)S(1)}, bf16[512,384]{0,1:T(8,128)(2,1)S(1)}, u32[]{:S(2)}, u32[]{:S(2)}) collective-permute-start(bf16[512,384]{0,1:T(8,128)(2,1)S(1)} %collective-permute-done.1), channel_id=1, source_target_pairs={{0,15},{1,0},{2,1},{3,2},{4,3},{5,4},{6,5},{7,6},{8,7},{9,8},{10,9... | collective-permute-start | bytes 1179656 | tf_op jit(solution)/shard_map/ppermute | solution.py:24
  184.5 62.8 %copy-start.5 = (bf16[512,384]{0,1:T(8,128)(2,1)}, bf16[512,384]{0,1:T(8,128)(2,1)S(1)}, u32[]{:S(2)}) copy-start(bf16[512,384]{0,1:T(8,128)(2,1)S(1)} %collective-permute-done.2) | copy-start | bytes 1179652
  184.5 64.4 %collective-permute-start.4 = (bf16[512,384]{0,1:T(8,128)(2,1)S(1)}, bf16[512,384]{0,1:T(8,128)(2,1)S(1)}, u32[]{:S(2)}, u32[]{:S(2)}) collective-permute-start(bf16[512,384]{0,1:T(8,128)(2,1)S(1)} %collective-permute-done.2), channel_id=1, source_target_pairs={{0,1},{1,2},{2,3},{3,4},{4,5},{5,6},{6,7},{7,8},{8,9},{9,10},{10,1... | collective-permute-start | bytes 1179656 | tf_op jit(solution)/shard_map/ppermute | solution.py:19
  237.1 11.9 %copy-start.1 = (bf16[512,6144]{1,0:T(8,128)(2,1)S(1)}, bf16[512,6144]{1,0:T(8,128)(2,1)}, u32[]{:S(2)}) copy-start(bf16[512,6144]{1,0:T(8,128)(2,1)} %all-gather.2.cloned.1.call-done) | copy-start | bytes 18874372
  247.3 7.5 %copy-start.8 = (bf16[512,384]{0,1:T(8,128)(2,1)}, bf16[512,384]{0,1:T(8,128)(2,1)S(1)}, u32[]{:S(2)}) copy-start(bf16[512,384]{0,1:T(8,128)(2,1)S(1)} %collective-permute-done.3) | copy-start | bytes 1179652
  247.3 8.2 %collective-permute-start.5 = (bf16[512,384]{0,1:T(8,128)(2,1)S(1)}, bf16[512,384]{0,1:T(8,128)(2,1)}, u32[]{:S(2)}, u32[]{:S(2)}) collective-permute-start(bf16[512,384]{0,1:T(8,128)(2,1)S(1)} %collective-permute-done.3), channel_id=1, source_target_pairs={{0,15},{1,0},{2,1},{3,2},{4,3},{5,4},{6,5},{7,6},{8,7},{9,8},{10,9... | collective-permute-start | bytes 1179656 | tf_op jit(solution)/shard_map/ppermute | solution.py:24
  248.9 5.9 %copy-start.9 = (bf16[512,384]{0,1:T(8,128)(2,1)}, bf16[512,384]{0,1:T(8,128)(2,1)S(1)}, u32[]{:S(2)}) copy-start(bf16[512,384]{0,1:T(8,128)(2,1)S(1)} %collective-permute-done.4) | copy-start | bytes 1179652
  248.9 12.1 %collective-permute-start.6 = (bf16[512,384]{0,1:T(8,128)(2,1)S(1)}, bf16[512,384]{0,1:T(8,128)(2,1)}, u32[]{:S(2)}, u32[]{:S(2)}) collective-permute-start(bf16[512,384]{0,1:T(8,128)(2,1)S(1)} %collective-permute-done.4), channel_id=1, source_target_pairs={{0,1},{1,2},{2,3},{3,4},{4,5},{5,6},{6,7},{7,8},{8,9},{9,10},{10,1... | collective-permute-start | bytes 1179656 | tf_op jit(solution)/shard_map/ppermute | solution.py:19
  255.5 86.2 %collective-permute-start.7 = (bf16[512,384]{0,1:T(8,128)(2,1)}, bf16[512,384]{0,1:T(8,128)(2,1)}, u32[]{:S(2)}, u32[]{:S(2)}) collective-permute-start(bf16[512,384]{0,1:T(8,128)(2,1)} %collective-permute-done.5), channel_id=1, source_target_pairs={{0,15},{1,0},{2,1},{3,2},{4,3},{5,4},{6,5},{7,6},{8,7},{9,8},{10,9... | collective-permute-start | bytes 1179656 | tf_op jit(solution)/shard_map/ppermute | solution.py:24
  261.0 83.7 %collective-permute-start.8 = (bf16[512,384]{0,1:T(8,128)(2,1)}, bf16[512,384]{0,1:T(8,128)(2,1)}, u32[]{:S(2)}, u32[]{:S(2)}) collective-permute-start(bf16[512,384]{0,1:T(8,128)(2,1)} %collective-permute-done.6), channel_id=1, source_target_pairs={{0,1},{1,2},{2,3},{3,4},{4,5},{5,6},{6,7},{7,8},{8,9},{9,10},{10,1... | collective-permute-start | bytes 1179656 | tf_op jit(solution)/shard_map/ppermute | solution.py:19
  334.4 43.3 %slice-start = ((s8[6291456]{0:T(1024)(128)(4,1)}), s8[2097152]{0:T(1024)(128)(4,1)S(1)}, s32[]{:S(2)}) async-start(s8[6291456]{0:T(1024)(128)(4,1)} %bitcast.25), calls=%async_computation.4 | async-start | bytes 4194304
  339.9 37.7 %copy-start.4 = (f32[256,512]{1,0:T(8,128)S(1)}, f32[256,512]{1,0:T(8,128)}, u32[]{:S(2)}) copy-start(f32[256,512]{1,0:T(8,128)} %convolution_multiply_fusion.2) | copy-start | bytes 1572868
  341.8 8.4 %collective-permute-start.9 = (bf16[512,384]{0,1:T(8,128)(2,1)}, bf16[512,384]{0,1:T(8,128)(2,1)S(1)}, u32[]{:S(2)}, u32[]{:S(2)}) collective-permute-start(bf16[512,384]{0,1:T(8,128)(2,1)} %collective-permute-done.7), channel_id=1, source_target_pairs={{0,15},{1,0},{2,1},{3,2},{4,3},{5,4},{6,5},{7,6},{8,7},{9,8},{10,9... | collective-permute-start | bytes 1179656 | tf_op jit(solution)/shard_map/ppermute | solution.py:24
  344.7 11.7 %collective-permute-start.10 = (bf16[512,384]{0,1:T(8,128)(2,1)}, bf16[512,384]{0,1:T(8,128)(2,1)S(1)}, u32[]{:S(2)}, u32[]{:S(2)}) collective-permute-start(bf16[512,384]{0,1:T(8,128)(2,1)} %collective-permute-done.8), channel_id=1, source_target_pairs={{0,1},{1,2},{2,3},{3,4},{4,5},{5,6},{6,7},{7,8},{8,9},{9,10},{10,1... | collective-permute-start | bytes 1179656 | tf_op jit(solution)/shard_map/ppermute | solution.py:19
  348.2 29.4 %slice-start.1 = ((s8[6291456]{0:T(1024)(128)(4,1)}), s8[4194304]{0:T(1024)(128)(4,1)S(1)}, s32[]{:S(2)}) async-start(s8[6291456]{0:T(1024)(128)(4,1)} %bitcast.25), calls=%async_computation.5 | async-start | bytes 8388608
  350.2 11.6 %collective-permute-start.11 = (bf16[512,384]{0,1:T(8,128)(2,1)S(1)}, bf16[512,384]{0,1:T(8,128)(2,1)S(1)}, u32[]{:S(2)}, u32[]{:S(2)}) collective-permute-start(bf16[512,384]{0,1:T(8,128)(2,1)S(1)} %collective-permute-done.9), channel_id=1, source_target_pairs={{0,15},{1,0},{2,1},{3,2},{4,3},{5,4},{6,5},{7,6},{8,7},{9,8},{10,9... | collective-permute-start | bytes 1179656 | tf_op jit(solution)/shard_map/ppermute | solution.py:24
  356.4 10.6 %collective-permute-start.12 = (bf16[512,384]{0,1:T(8,128)(2,1)S(1)}, bf16[512,384]{0,1:T(8,128)(2,1)S(1)}, u32[]{:S(2)}, u32[]{:S(2)}) collective-permute-start(bf16[512,384]{0,1:T(8,128)(2,1)S(1)} %collective-permute-done.10), channel_id=1, source_target_pairs={{0,1},{1,2},{2,3},{3,4},{4,5},{5,6},{6,7},{7,8},{8,9},{9,10},{10,1... | collective-permute-start | bytes 1179656 | tf_op jit(solution)/shard_map/ppermute | solution.py:19
  361.7 9.7 %collective-permute-start.13 = (bf16[512,384]{0,1:T(8,128)(2,1)S(1)}, bf16[512,384]{0,1:T(8,128)(2,1)S(1)}, u32[]{:S(2)}, u32[]{:S(2)}) collective-permute-start(bf16[512,384]{0,1:T(8,128)(2,1)S(1)} %collective-permute-done.11), channel_id=1, source_target_pairs={{0,15},{1,0},{2,1},{3,2},{4,3},{5,4},{6,5},{7,6},{8,7},{9,8},{10,9... | collective-permute-start | bytes 1179656 | tf_op jit(solution)/shard_map/ppermute | solution.py:24
  367.0 9.9 %collective-permute-start.14 = (bf16[512,384]{0,1:T(8,128)(2,1)S(1)}, bf16[512,384]{0,1:T(8,128)(2,1)S(1)}, u32[]{:S(2)}, u32[]{:S(2)}) collective-permute-start(bf16[512,384]{0,1:T(8,128)(2,1)S(1)} %collective-permute-done.12), channel_id=1, source_target_pairs={{0,1},{1,2},{2,3},{3,4},{4,5},{5,6},{6,7},{7,8},{8,9},{9,10},{10,1... | collective-permute-start | bytes 1179656 | tf_op jit(solution)/shard_map/ppermute | solution.py:19
  377.6 8.1 %copy-start.2 = (f32[512,512]{1,0:T(8,128)S(1)}, f32[512,512]{1,0:T(8,128)}, u32[]{:S(2)}) copy-start(f32[512,512]{1,0:T(8,128)} %all-reduce.2.cloned.1.call-done) | copy-start | bytes 3145732
Sparse Core Ops, SparseCore 0:
  23.1 137.3 reduce-scatter.1
  162.6 74.4 all-gather.1
  240.5 93.7 all-reduce.1
